TPU v7x, 128 devices: a whole 4x4x4 slice. The times are simulated.
128 devices in a mesh: seq: 32 (over x, y_hi, z), mp: 4 (over y_lo, core).
Axes of the slice: x: 4, y: 4 (y_hi: 2, y_lo: 2; y = y_hi * 2 + y_lo), z: 4, core: 2. Of those that a mesh axis runs over, the one named last changes fastest.
Arguments:
- hidden_in: bfloat16 [8192, 1536], P('seq', 'mp'), may hold values from -6 to 6
- wq: bfloat16 [1536, 1536], P('seq', 'mp'), may hold values from -1 to 1
- wkv: bfloat16 [1536, 512], P('seq'), may hold values from -0.15625 to 0.15625
- wo: bfloat16 [1536, 1536], P('mp', 'seq'), may hold values from -0.15625 to 0.15625
- lengths: int32 [3], replicated, may hold values from 1 to 6144, 8192 in all
- routes: int32 [8192, 4], P('seq'), may hold values from 0 to 31, all different within a row; in each aligned block of 256 rows (0 to 255, 256 to 511, ...) at most 64 rows name the same one
- gate_logits: float32 [8192, 4], P('seq'), may hold values from -6 to 6
- expert_gate: bfloat16 [32, 768, 1536], P('seq', 'mp'), may hold values from -0.15625 to 0.15625
- expert_up: bfloat16 [32, 768, 1536], P('seq', 'mp'), may hold values from -0.15625 to 0.15625
- expert_down: bfloat16 [32, 768, 1536], P('seq', 'mp'), may hold values from -0.21875 to 0.21875
Outputs:
- layer_out: bfloat16 [8192, 1536], P('seq', 'mp')
Inputs may be any that keep to these rules, and one draw needn't show every extreme that they name: `lengths`: sum to 8192; the longest is exactly 6144. `routes`: a token's 4 experts differ; among the rows of one device no expert is named more than 64 times, a bound that some block reaches.
All inputs are finite; a program needn't handle non-finite values.
Results may differ from a plain program's by a relative error of at most 0.018.
Values may be sent and summed in bfloat16 or wider, within the bound.
No kernel may reach another device: no remote copies, remote signals or barrier semaphores. Data moves between devices by JAX's collectives and lax.ppermute only.
A program may use at most 128 MiB of HBM per device.

v0:
```python
import math
import jax
import jax.numpy as jnp
from jax import lax
from jax.sharding import PartitionSpec as P

D = 1536
HQ = 12
KVH = 2
HD = 128
WINDOW = 4096
ROPE_BASE = 1500000.0
EPSILON = 1e-06


def prompt_ids(index, lengths):
    first_end = lengths[0]
    second_end = lengths[0] + lengths[1]
    prompt = (index >= first_end).astype(jnp.int32) + (index >= second_end).astype(jnp.int32)
    begin = jnp.where(index >= second_end, second_end, jnp.where(index >= first_end, first_end, 0))
    return (prompt, index - begin)


def rotary(values, position):
    half_dim = values.shape[-1] // 2
    freqs = jnp.exp(
        jnp.arange(half_dim, dtype=jnp.float32) * (-2.0 * math.log(ROPE_BASE) / values.shape[-1])
    )
    angles = position.astype(jnp.float32)[:, None] * freqs[None, :]
    cosine = jnp.cos(angles)[:, None, :]
    sine = jnp.sin(angles)[:, None, :]
    front = values[..., :half_dim]
    latter = values[..., half_dim:]
    return jnp.concatenate(
        [front * cosine - latter * sine, latter * cosine + front * sine], axis=-1
    )


def attend(carry, piece, queries, query_index, lengths):
    peak, total, accum = carry
    key_rows = piece[:, 0, :]
    value_rows = piece[:, 1, :].astype(jnp.float32)
    scores = jnp.einsum(
        "hqd,kd->hqk", queries, key_rows, preferred_element_type=jnp.float32
    ) * HD ** (-0.5)
    key_index = jnp.arange(piece.shape[0], dtype=jnp.int32)
    query_prompt, _ = prompt_ids(query_index, lengths)
    key_prompt, _ = prompt_ids(key_index, lengths)
    spacing = query_index[:, None] - key_index[None, :]
    allowed = (
        (query_prompt[:, None] == key_prompt[None, :])
        & (spacing >= 0)
        & (spacing < WINDOW)
        & (key_index[None, :] >= 0)
    )[None]
    masked = jnp.where(allowed, scores, -1e30)
    new_peak = jnp.maximum(peak, jnp.max(masked, axis=-1))
    weights = jnp.where(allowed, jnp.exp(masked - new_peak[..., None]), 0.0)
    total = jnp.sum(weights, axis=-1)
    accum = jnp.einsum("hqk,kd->hqd", weights, value_rows)
    return (new_peak, total, accum)


def local(
    hidden_in, wq, wkv, wo, lengths, routes, gate_logits, expert_gate, expert_up, expert_down
):
    tok_rows = hidden_in.shape[0]
    seq_index = lax.axis_index("seq")
    mp_index = lax.axis_index("mp")
    seq_count = lax.axis_size("seq")
    whole = lax.all_gather(hidden_in, "mp", axis=1, tiled=True)
    whole_f = whole.astype(jnp.float32)
    normed = (
        whole_f * lax.rsqrt(jnp.sum(whole_f * whole_f, axis=-1, keepdims=True) / D + EPSILON)
    ).astype(jnp.bfloat16)
    heads_here = wq.shape[1] // HD
    query_lin = jnp.dot(
        normed, lax.all_gather(wq, "seq", axis=0, tiled=True), preferred_element_type=jnp.float32
    )
    kv_lin = jnp.dot(
        normed, lax.all_gather(wkv, "seq", axis=0, tiled=True), preferred_element_type=jnp.float32
    )
    own_index = seq_index * tok_rows + jnp.arange(tok_rows, dtype=jnp.int32)
    _, own_pos = prompt_ids(own_index, lengths)
    queries = (
        rotary(query_lin.reshape(tok_rows, heads_here, HD), own_pos)
        .astype(jnp.bfloat16)
        .transpose(1, 0, 2)
    )
    kv_group = mp_index * heads_here // (HQ // KVH)
    key_all = kv_lin[:, : KVH * HD].reshape(tok_rows, KVH, HD)
    value_all = kv_lin[:, KVH * HD :].reshape(tok_rows, KVH, HD)
    key_own = rotary(lax.dynamic_slice_in_dim(key_all, kv_group, 1, 1), own_pos)[:, 0, :]
    value_own = lax.dynamic_slice_in_dim(value_all, kv_group, 1, 1)[:, 0, :]
    kv_own = jnp.stack([key_own.astype(jnp.bfloat16), value_own.astype(jnp.bfloat16)], axis=1)
    start_attn = (
        jnp.full((heads_here, tok_rows), -1e30, jnp.float32),
        jnp.zeros((heads_here, tok_rows), jnp.float32),
        jnp.zeros((heads_here, tok_rows, HD), jnp.float32),
    )
    carry = attend(
        start_attn, lax.all_gather(kv_own, "seq", axis=0, tiled=True), queries, own_index, lengths
    )
    _, total, accum = carry
    attended = (
        (accum / total[..., None])
        .transpose(1, 0, 2)
        .reshape(tok_rows, heads_here * HD)
        .astype(jnp.bfloat16)
    )
    partial_out = jnp.dot(
        attended, lax.all_gather(wo, "seq", axis=1, tiled=True), preferred_element_type=jnp.float32
    )
    attn_mine = lax.psum_scatter(
        partial_out.astype(jnp.bfloat16), "mp", scatter_dimension=1, tiled=True
    ).astype(jnp.float32)
    residual = (hidden_in.astype(jnp.float32) + attn_mine).astype(jnp.bfloat16)
    residual_f = residual.astype(jnp.float32)
    square_sum = lax.psum(jnp.sum(residual_f * residual_f, axis=-1), "mp")
    moe_local = (residual_f * lax.rsqrt(square_sum / D + EPSILON)[:, None]).astype(jnp.bfloat16)
    local_experts = expert_gate.shape[0]
    experts = seq_count * local_experts
    top_count = routes.shape[1]
    capacity = 2 * tok_rows * top_count // experts
    flat_ids = routes.reshape(-1)
    one_hot = (flat_ids[:, None] == jnp.arange(experts, dtype=jnp.int32)[None, :]).astype(jnp.int32)
    earlier_count = jnp.sum((jnp.cumsum(one_hot, axis=0) - one_hot) * one_hot, axis=1)
    slot_index = flat_ids * capacity + earlier_count
    source_row = jnp.arange(tok_rows * top_count, dtype=jnp.int32) // top_count
    full_rows = lax.all_gather(moe_local, "mp", axis=1, tiled=True)
    buffer = (
        jnp.zeros((experts * capacity, full_rows.shape[1]), jnp.bfloat16)
        .at[slot_index]
        .set(full_rows[source_row])
    )
    arrived = lax.all_to_all(
        buffer.reshape(experts, capacity, full_rows.shape[1]),
        "seq",
        split_axis=0,
        concat_axis=0,
        tiled=True,
    )
    arrived = arrived.reshape(seq_count, local_experts, capacity, D)
    gate_act = jnp.einsum(
        "secd,efd->secf", arrived, expert_gate, preferred_element_type=jnp.float32
    )
    up_act = jnp.einsum("secd,efd->secf", arrived, expert_up, preferred_element_type=jnp.float32)
    active = (jnp.maximum(gate_act, 0.0) * up_act).astype(jnp.bfloat16)
    partial_expert = jnp.einsum(
        "secf,efd->secd", active, expert_down, preferred_element_type=jnp.float32
    )
    summed = lax.psum_scatter(
        partial_expert.astype(jnp.bfloat16), "mp", scatter_dimension=3, tiled=True
    )
    feature_part = summed.shape[3]
    returned = lax.all_to_all(
        summed.reshape(seq_count * local_experts, capacity, feature_part),
        "seq",
        split_axis=0,
        concat_axis=0,
        tiled=True,
    )
    picked_back = returned.reshape(experts * capacity, feature_part)[slot_index]
    gate_weights = jax.nn.softmax(gate_logits, axis=-1)
    weighted = picked_back.astype(jnp.float32) * gate_weights.reshape(-1)[:, None]
    moe_total = jnp.sum(weighted.reshape(tok_rows, top_count, feature_part), axis=1)
    return (residual_f + moe_total).astype(jnp.bfloat16)


def solution(mesh):
    return jax.shard_map(
        local,
        mesh=mesh,
        in_specs=(
            P("seq", "mp"),
            P("seq", "mp"),
            P("seq", None),
            P("mp", "seq"),
            P(),
            P("seq", None),
            P("seq", None),
            P("seq", "mp", None),
            P("seq", "mp", None),
            P("seq", "mp", None),
        ),
        out_specs=P("seq", "mp"),
        check_vma=False,
    )
```

profile of v0, /device:TPU:0, one launch (start us, length us, event | category | flops | bytes accessed | tf_op | source)
XLA Modules:
  0.0 610.1 jit_solution(7796226806283322392)
XLA Ops:
  6.5 0.7 all-gather.7.cloned.1.call-update
  7.3 0.7 all-gather.5.cloned.1.call-update
  8.1 1.3 fusion.57
  10.7 0.7 subtract_convert_fusion.1
  11.4 9.0 %all_gather.18 = bf16[256,1536]{1,0:T(8,128)(2,1)S(1)} all-gather(bf16[256,384]{1,0:T(8,128)(2,1)} %param.10), channel_id=1, replica_groups=mesh['seq'=32,'mp'=4] {'mp'}, dimensions={1}, use_global_device_ids=true | all-gather | bytes 983040 | tf_op jit(solution)/shard_map/all_gather | solution.py:71
  20.4 0.2 fusion.16
  20.7 60.8 %all-gather.7.cloned.1.call-done = bf16[1536,512]{1,0:T(8,128)(2,1)} async-done(((bf16[48,512]{1,0:T(8,128)(2,1)}), bf16[1536,512]{1,0:T(8,128)(2,1)}) %all-gather.7.cloned.1.call-update) | async-done | bytes 1572880 | tf_op jit(solution)/shard_map/all_gather | solution.py:81
  81.5 2.0 fusion.29
  83.6 0.1 copy.44
  83.7 0.1 copy.45
  83.8 0.3 fusion.44
  84.2 0.6 pad_maximum_fusion
  84.9 0.5 all-gather.11.cloned.1.call-update
  85.4 1.2 multiply_cosine_fusion
  86.7 0.7 convert_add_fusion.2
  87.4 0.7 convert_add_fusion.1
  88.1 2.7 fusion.11
  90.7 57.7 %all-gather.5.cloned.1.call-done = bf16[1536,384]{1,0:T(8,128)(2,1)} async-done(((bf16[48,384]{1,0:T(8,128)(2,1)}), bf16[1536,384]{1,0:T(8,128)(2,1)}) %all-gather.5.cloned.1.call-update) | async-done | bytes 1179664 | tf_op jit(solution)/shard_map/all_gather | solution.py:78
  148.5 1.9 fusion.31
  150.4 0.7 fusion.56
  151.1 0.2 copy.60
  151.3 1.1 copy.61
  152.4 1.8 subtract_convert_fusion
  154.2 74.4 %all-gather.9.cloned.1.call-done = bf16[8192,2,128]{0,2,1:T(8,128)(2,1)} async-done(((bf16[256,2,128]{0,2,1:T(8,128)(2,1)}), bf16[8192,2,128]{0,2,1:T(8,128)(2,1)}) %all-gather.9.cloned.1.call-update) | async-done | bytes 4194320 | tf_op jit(solution)/shard_map/all_gather | solution.py:102
  228.5 12.2 %fusion = (f32[3,256]{1,0:T(4,128)S(1)}, f32[3,256,8192]{2,1,0:T(8,128)}) fusion(pred[256,8192]{1,0:T(8,128)(4,1)S(1)} %fusion.11, bf16[8192,2,128]{0,2,1:T(8,128)(2,1)} %all-gather.9.cloned.1.call-done, bf16[256,3,64]{2,0,1:T(8,128)(2,1)} %get-tuple-element.6, bf16[256,3,64]{2,0,1:T(8,128)(2,1)} %get-tuple-element.5), kind=kOutput, calls=%fused_computation.5 | convolution fusion | flops 1629879552 | bytes 29756416 | tf_op jit(solution)/shard_map/hqd,kd->hqk/dot_general | solution.py:43
  240.8 12.5 %fusion.1 = f32[3,256]{1,0:T(4,128)S(1)} fusion(f32[3,256,8192]{2,1,0:T(8,128)} %get-tuple-element.16, f32[3,256]{1,0:T(4,128)S(1)} %broadcast_maximum_fusion, pred[256,8192]{1,0:T(8,128)(4,1)S(1)} %fusion.11), kind=kLoop, calls=%fused_computation.6 | loop fusion | flops 31456512 | bytes 27269120 | tf_op jit(solution)/shard_map/reduce_sum | solution.py:59
  253.3 11.8 %fusion.20 = bf16[256,3,128]{0,2,1:T(8,128)(2,1)S(1)} fusion(bf16[8192,2,128]{0,2,1:T(8,128)(2,1)S(1)} %copy-done.5, f32[3,256,8192]{2,1,0:T(8,128)} %get-tuple-element.16, f32[3,256]{1,0:T(4,128)S(1)} %broadcast_maximum_fusion, pred[256,8192]{1,0:T(8,128)(4,1)S(1)} %fusion.11, f32[256,3]{0,1:T(4,128)S(1)} %bitcast.108), kind=kOutput, calls=%fused_computation.34 | convolution fusion | flops 1635975168 | bytes 29564928 | tf_op jit(solution)/shard_map/hqk,kd->hqd/dot_general | solution.py:60
  265.1 33.9 %all-gather.11.cloned.1.call-done = bf16[384,1536]{0,1:T(8,128)(2,1)} async-done(((bf16[384,48]{0,1:T(8,128)(2,1)}), bf16[384,1536]{0,1:T(8,128)(2,1)}) %all-gather.11.cloned.1.call-update) | async-done | bytes 1179664 | tf_op jit(solution)/shard_map/all_gather | solution.py:112
  299.0 1.9 convolution_convert_fusion
  300.9 1.2 copy.56
  302.1 0.2 reduce-scatter.9.cloned.1.call-start
  302.3 0.1 copy.48
  302.5 0.1 eq.49
  302.6 0.1 eq.45
  302.7 9.0 %reduce-window.6 = s32[32,8,128]{2,1,0:T(8,128)S(1)} reduce-window(s32[32,8,128]{2,1,0:T(8,128)S(1)} %fusion.38, s32[]{:T(128)} %constant.26.clone.1), window={size=1x1x128 pad=0_0x0_0x127_0}, to_apply=%region_4.5 | reduce-window | flops 4161536 | bytes 262148 | tf_op jit(solution)/shard_map/reduce-window
  311.8 0.1 slice.65
  311.9 0.1 copy.50
  312.0 0.1 copy.51
  312.1 0.1 copy.47
  312.3 0.1 mul.183
  312.4 0.1 broadcast_add_fusion
  312.6 5.7 reduce-scatter.7.cloned.1.call-done
  318.3 1.1 copy.57
  319.4 0.1 fusion.26
  319.5 5.9 psum.7
  325.4 0.1 fusion.27
  325.5 8.7 %all_gather.23 = bf16[256,1536]{1,0:T(8,128)(2,1)S(1)} all-gather(bf16[256,384]{1,0:T(8,128)(2,1)S(1)} %fusion.27), channel_id=1, replica_groups=mesh['seq'=32,'mp'=4] {'mp'}, dimensions={1}, use_global_device_ids=true | all-gather | bytes 983040 | tf_op jit(solution)/shard_map/all_gather | solution.py:130
  334.3 19.7 %scatter_custom_fusion = bf16[2048,1536]{1,0:T(8,128)(2,1)} fusion(s32[1024]{0:T(1024)S(1)} %bitcast.105, bf16[256,1536]{1,0:T(8,128)(2,1)S(1)} %all_gather.23, s32[1024]{0:T(1024)S(1)} %broadcast_clamp_fusion.1, bf16[]{:T(256)} %constant.75.clone.1), kind=kCustom, calls=%fused_computation.19 | custom fusion | bytes 6291458 | tf_op jit(solution)/shard_map/scatter | solution.py:134
  354.0 84.0 %all_to_all.10 = bf16[32,64,1536]{2,1,0:T(8,128)(2,1)S(1)} all-to-all(bf16[32,64,1536]{2,1,0:T(8,128)(2,1)} %bitcast.93), channel_id=1, replica_groups=mesh['seq'=32,'mp'=4] {'seq'}, dimensions={0} | all-to-all | bytes 12582912 | tf_op jit(solution)/shard_map/all_to_all | solution.py:136
  438.0 2.7 copy-done.1
  440.6 3.2 fusion.24
  443.8 12.3 %convert_bitcast_fusion = bf16[32,1,64,1536]{3,2,0,1:T(8,128)(2,1)} fusion(f32[32,64,192]{2,1,0:T(8,128)} %fusion.24, bf16[32,64,1536]{2,1,0:T(8,128)(2,1)} %copy-done.1, bf16[1,192,1536]{2,1,0:T(8,128)(2,1)S(1)} %copy-done, bf16[1,192,1536]{2,1,0:T(8,128)(2,1)S(1)} %copy-done.7), kind=kOutput, calls=%fused_computation.18 | convolution fusion | flops 2420244480 | bytes 15335424 | tf_op jit(solution)/shard_map/secf,efd->secd/dot_general | solution.py:149
  456.1 18.4 %copy.58 = bf16[32,1,64,1536]{2,0,1,3:T(8,128)(2,1)} copy(bf16[32,1,64,1536]{3,2,0,1:T(8,128)(2,1)} %convert_bitcast_fusion) | data formatting | bytes 12582912
  474.5 17.9 %reshape.397 = bf16[1536,2048]{1,0:T(8,128)(2,1)} reshape(bf16[1536,1,32,64]{3,2,1,0:T(8,128)(2,1)} %bitcast.91) | data formatting | bytes 12582912
  492.4 60.4 %reduce-scatter.9.cloned.1.call-done = bf16[384,2048]{1,0:T(8,128)(2,1)} async-done(((bf16[1536,2048]{1,0:T(8,128)(2,1)}), bf16[384,2048]{1,0:T(8,128)(2,1)}) %reduce-scatter.9.cloned.1.call-update) | async-done | bytes 1572880
  552.8 5.7 reshape.398
  558.5 5.5 copy.59
  564.0 9.4 %all-to-all-start.1 = ((bf16[32,64,384]{2,1,0:T(8,128)(2,1)}), bf16[32,64,384]{2,1,0:T(8,128)(2,1)S(1)}, u32[]{:S(2)}, u32[]{:S(2)}) async-start(bf16[32,64,384]{2,1,0:T(8,128)(2,1)} %bitcast.95), calls=%async_computation.1 | async-start | bytes 3145728 | tf_op jit(solution)/shard_map/all_to_all | solution.py:156
  573.5 0.1 copy.52
  573.6 23.2 %all-to-all-done.1 = bf16[32,64,384]{2,1,0:T(8,128)(2,1)S(1)} async-done(((bf16[32,64,384]{2,1,0:T(8,128)(2,1)}), bf16[32,64,384]{2,1,0:T(8,128)(2,1)S(1)}, u32[]{:S(2)}, u32[]{:S(2)}) %all-to-all-start.1) | async-done | bytes 1572896 | tf_op jit(solution)/shard_map/all_to_all | solution.py:156
  596.8 3.9 gather_fusion
  600.7 0.4 reshape.365
  601.1 1.0 multiply_reduce_fusion
  602.1 0.7 fusion.28
  (42 shorter events, 0.5 us)
Async XLA Ops:
  6.5 437.3 %copy-start = (bf16[1,192,1536]{2,1,0:T(8,128)(2,1)S(1)}, bf16[1,192,1536]{2,1,0:T(8,128)(2,1)}, u32[]{:S(2)}) copy-start(bf16[1,192,1536]{2,1,0:T(8,128)(2,1)} %param.19) | copy-start | bytes 1769476
  6.5 74.9 %all-gather.7.cloned.1.call-start = ((), (), s32[]{:S(2)}) async-start(), calls=%async_computation.5 | async-start | bytes 1622016 | tf_op jit(solution)/shard_map/all_gather | solution.py:81
  7.3 141.2 %all-gather.5.cloned.1.call-start = ((), (), s32[]{:S(2)}) async-start(), calls=%async_computation.4 | async-start | bytes 1216512 | tf_op jit(solution)/shard_map/all_gather | solution.py:78
  8.0 220.5 %all-gather.9.cloned.1.call-start = ((), (), s32[]{:S(2)}) async-start(), calls=%async_computation.6 | async-start | bytes 4325376 | tf_op jit(solution)/shard_map/all_gather | solution.py:102
  84.8 214.2 %all-gather.11.cloned.1.call-start = ((), (), s32[]{:S(2)}) async-start(), calls=%async_computation.7 | async-start | bytes 1216512 | tf_op jit(solution)/shard_map/all_gather | solution.py:112
  85.4 232.9 %reduce-scatter.7.cloned.1.call-start = ((), (), s32[]{:S(2)}) async-start(), calls=%async_computation.8 | async-start | bytes 983040
  240.8 12.5 %copy-start.5 = (bf16[8192,2,128]{0,2,1:T(8,128)(2,1)S(1)}, bf16[8192,2,128]{0,2,1:T(8,128)(2,1)}, u32[]{:S(2)}) copy-start(bf16[8192,2,128]{0,2,1:T(8,128)(2,1)} %all-gather.9.cloned.1.call-done) | copy-start | bytes 12582916
  265.1 37.2 %copy-start.4 = (s32[256,4]{0,1:T(4,128)S(1)}, s32[256,4]{0,1:T(4,128)}, u32[]{:S(2)}) copy-start(s32[256,4]{0,1:T(4,128)} %param.15) | copy-start | bytes 12292
  265.1 54.2 %copy-start.2 = (bf16[256,384]{1,0:T(8,128)(2,1)S(1)}, bf16[256,384]{1,0:T(8,128)(2,1)}, u32[]{:S(2)}) copy-start(bf16[256,384]{1,0:T(8,128)(2,1)} %param.10) | copy-start | bytes 589828
  302.1 250.7 %reduce-scatter.9.cloned.1.call-start = ((), (), s32[]{:S(2)}) async-start(), calls=%async_computation.9 | async-start | bytes 7864320
  354.0 86.7 %copy-start.6 = (bf16[1,192,1536]{2,1,0:T(8,128)(2,1)S(1)}, bf16[1,192,1536]{2,1,0:T(8,128)(2,1)}, u32[]{:S(2)}) copy-start(bf16[1,192,1536]{2,1,0:T(8,128)(2,1)} %param.17) | copy-start | bytes 1769476
  438.0 2.7 copy-start.1
  440.6 3.2 copy-start.7
  558.5 14.8 %copy-start.3 = (f32[256,4]{0,1:T(4,128)S(1)}, f32[256,4]{0,1:T(4,128)}, u32[]{:S(2)}) copy-start(f32[256,4]{0,1:T(4,128)} %param.16) | copy-start | bytes 12292
  564.0 32.8 %all-to-all-start.1 = ((bf16[32,64,384]{2,1,0:T(8,128)(2,1)}), bf16[32,64,384]{2,1,0:T(8,128)(2,1)S(1)}, u32[]{:S(2)}, u32[]{:S(2)}) async-start(bf16[32,64,384]{2,1,0:T(8,128)(2,1)} %bitcast.95), calls=%async_computation.1 | async-start | bytes 3145728 | tf_op jit(solution)/shard_map/all_to_all | solution.py:156
Sparse Core Ops, SparseCore 0:
  10.4 71.0 all-gather.6
  84.4 63.9 all-gather.4
  151.3 77.2 all-gather.8
  231.4 67.6 all-gather.10
  302.2 15.9 reduce-scatter.6
  492.6 60.2 reduce-scatter.8
where the time goes:
time: 620 us; the launch traced here: 610 us
  waiting for transfers between devices  318 us (51%)
  blocking collectives  108 us (17%)
  local copies, waits for them, and re-layouts  81 us (13%)
  matrix products  45.3 us (7%)
  other arithmetic  32.8 us (5%)
  between operations  15.5 us (2%)
  starting transfers between devices  9.75 us (2%)
    all_to_all x1, blocking collectives, local(): lax.all_to_all(buffer.reshape(experts, capacity, full_rows.shape[1]), 'se...  84 us
    all_gather x1, waiting for transfers between devices, local(): lax.all_gather(kv_own, 'seq', axis=0, tiled=True)  74.4 us
    unnamed x8, waiting for transfers between devices  68 us
    all_gather x1, waiting for transfers between devices, local(): lax.all_gather(wkv, 'seq', axis=0, tiled=True)  60.8 us
    all_gather x1, waiting for transfers between devices, local(): lax.all_gather(wq, 'seq', axis=0, tiled=True)  57.7 us
    unnamed x25, local copies, waits for them, and re-layouts  53.8 us
    all_gather x1, waiting for transfers between devices, local(): lax.all_gather(wo, 'seq', axis=1, tiled=True)  33.9 us
    all_to_all x1, waiting for transfers between devices, local(): lax.all_to_all(summed.reshape(seq_count * local_experts, capacity, featur...  23.2 us
  transfers between devices with their start and end apart: 7, of which 7 were waited for; matrix products, arithmetic and copies ran while one was open for 10% of the time, Pallas kernels for 0%

commit v1 on v0

--- a/solution.py
+++ b/solution.py
@@ -78,7 +78,11 @@
         normed, lax.all_gather(wq, "seq", axis=0, tiled=True), preferred_element_type=jnp.float32
     )
     kv_lin = jnp.dot(
-        normed, lax.all_gather(wkv, "seq", axis=0, tiled=True), preferred_element_type=jnp.float32
+        normed,
+        jnp.concatenate(
+            lax.all_to_all(jnp.stack([wkv] * lax.axis_size("seq")), "seq", 0, 0), axis=0
+        ),
+        preferred_element_type=jnp.float32,
     )
     own_index = seq_index * tok_rows + jnp.arange(tok_rows, dtype=jnp.int32)
     _, own_pos = prompt_ids(own_index, lengths)

time: 620 us -> 556 us (0.90)
  waiting for transfers between devices: 318 us -> 237 us
  starting transfers between devices: 9.75 us -> 20.9 us
  blocking collectives: 108 us -> 119 us
    all_gather x1 -> x0, waiting for transfers between devices: 60.8 us -> none  [local(): lax.all_gather(wkv, 'seq', axis=0, tiled=True)]
    all_gather x1, waiting for transfers between devices: 57.7 us -> 37.9 us  [local(): lax.all_gather(wq, 'seq', axis=0, tiled=True)]
    all_gather x1, blocking collectives: 8.98 us -> 20.6 us  [local(): whole = lax.all_gather(hidden_in, 'mp', axis=1, tiled=True)]
    all_to_all x0 -> x1, starting transfers between devices: none -> 10.9 us  [local(): lax.all_to_all(jnp.stack([wkv] * lax.axis_size('seq')), 'seq', 0, 0)]
    unnamed x8 -> x7, waiting for transfers between devices: 68 us -> 67.8 us
    unnamed x25 -> x29, local copies, waits for them, and re-layouts: 53.8 us -> 53.8 us
  transfers between devices with their start and end apart: 7 -> 7, of which waited for: 7 -> 6; matrix products, arithmetic and copies ran while one was open for 10% -> 11% of each run, Pallas kernels for 0% -> 0%
where the time goes in v1:
time: 556 us; the launch traced here: 552 us
  waiting for transfers between devices  237 us (43%)
  blocking collectives  119 us (21%)
  local copies, waits for them, and re-layouts  82.4 us (15%)
  matrix products  43.9 us (8%)
  other arithmetic  32.8 us (6%)
  starting transfers between devices  20.9 us (4%)
  between operations  15.1 us (3%)
    all_to_all x1, blocking collectives, local(): lax.all_to_all(buffer.reshape(experts, capacity, full_rows.shape[1]), 'se...  83.9 us
    all_gather x1, waiting for transfers between devices, local(): lax.all_gather(kv_own, 'seq', axis=0, tiled=True)  74.4 us
    unnamed x7, waiting for transfers between devices  67.8 us
    unnamed x29, local copies, waits for them, and re-layouts  53.8 us
    all_gather x1, waiting for transfers between devices, local(): lax.all_gather(wq, 'seq', axis=0, tiled=True)  37.9 us
    all_gather x1, waiting for transfers between devices, local(): lax.all_gather(wo, 'seq', axis=1, tiled=True)  34.1 us
    all_to_all x1, waiting for transfers between devices, local(): lax.all_to_all(summed.reshape(seq_count * local_experts, capacity, featur...  23.2 us
    all_gather x1, blocking collectives, local(): whole = lax.all_gather(hidden_in, 'mp', axis=1, tiled=True)  20.6 us
  transfers between devices with their start and end apart: 7, of which 6 were waited for; matrix products, arithmetic and copies ran while one was open for 11% of the time, Pallas kernels for 0%

profile of v1, /device:TPU:0, one launch (start us, length us, event | category | flops | bytes accessed | tf_op | source)
XLA Modules:
  0.0 551.7 jit_solution(7780043015228748415)
XLA Ops:
  6.5 0.7 all-gather.4.cloned.1.call-update
  7.3 2.1 stack.4
  9.4 10.9 %all-to-all-start = ((bf16[32,48,512]{2,1,0:T(8,128)(2,1)}), bf16[32,48,512]{2,1,0:T(8,128)(2,1)S(1)}, u32[]{:S(2)}, u32[]{:S(2)}) async-start(bf16[32,48,512]{2,1,0:T(8,128)(2,1)} %stack.4), calls=%async_computation | async-start | bytes 3145728 | tf_op jit(solution)/shard_map/all_to_all | solution.py:83
  20.4 0.6 fusion.57
  22.3 0.7 subtract_convert_fusion.1
  23.0 20.6 %all_gather.15 = bf16[256,1536]{1,0:T(8,128)(2,1)S(1)} all-gather(bf16[256,384]{1,0:T(8,128)(2,1)S(1)} %copy-done.2), channel_id=1, replica_groups=mesh['seq'=32,'mp'=4] {'mp'}, dimensions={1}, use_global_device_ids=true | all-gather | bytes 983040 | tf_op jit(solution)/shard_map/all_gather | solution.py:71
  43.6 0.2 fusion.16
  43.8 0.6 fusion.29
  44.5 0.1 copy.44
  44.6 0.1 copy.45
  44.7 0.3 fusion.44
  45.1 0.6 pad_maximum_fusion
  45.8 0.7 all-gather.8.cloned.1.call-update
  46.5 0.5 reduce-scatter.7.cloned.1.call-start
  47.0 1.2 multiply_cosine_fusion
  48.2 0.7 convert_add_fusion.2
  48.9 0.7 convert_add_fusion.1
  49.6 2.7 fusion.11
  52.3 37.9 %all-gather.4.cloned.1.call-done = bf16[1536,384]{1,0:T(8,128)(2,1)} async-done(((bf16[48,384]{1,0:T(8,128)(2,1)}), bf16[1536,384]{1,0:T(8,128)(2,1)}) %all-gather.4.cloned.1.call-update) | async-done | bytes 1179664 | tf_op jit(solution)/shard_map/all_gather | solution.py:78
  90.2 1.9 fusion.31
  92.1 0.7 fusion.56
  92.8 0.2 copy.60
  92.9 1.1 copy.61
  94.0 1.8 subtract_convert_fusion
  95.9 74.4 %all-gather.6.cloned.1.call-done = bf16[8192,2,128]{0,2,1:T(8,128)(2,1)} async-done(((bf16[256,2,128]{0,2,1:T(8,128)(2,1)}), bf16[8192,2,128]{0,2,1:T(8,128)(2,1)}) %all-gather.6.cloned.1.call-update) | async-done | bytes 4194320 | tf_op jit(solution)/shard_map/all_gather | solution.py:106
  170.2 12.2 %fusion = (f32[3,256]{1,0:T(4,128)S(1)}, f32[3,256,8192]{2,1,0:T(8,128)}) fusion(pred[256,8192]{1,0:T(8,128)(4,1)S(1)} %fusion.11, bf16[8192,2,128]{0,2,1:T(8,128)(2,1)} %all-gather.6.cloned.1.call-done, bf16[256,3,64]{2,0,1:T(8,128)(2,1)} %get-tuple-element.6, bf16[256,3,64]{2,0,1:T(8,128)(2,1)} %get-tuple-element.5), kind=kOutput, calls=%fused_computation.5 | convolution fusion | flops 1629879552 | bytes 29756416 | tf_op jit(solution)/shard_map/hqd,kd->hqk/dot_general | solution.py:43
  182.4 12.5 %fusion.1 = f32[3,256]{1,0:T(4,128)S(1)} fusion(f32[3,256,8192]{2,1,0:T(8,128)} %get-tuple-element.16, f32[3,256]{1,0:T(4,128)S(1)} %broadcast_maximum_fusion, pred[256,8192]{1,0:T(8,128)(4,1)S(1)} %fusion.11), kind=kLoop, calls=%fused_computation.6 | loop fusion | flops 31456512 | bytes 27269120 | tf_op jit(solution)/shard_map/reduce_sum | solution.py:59
  195.0 11.8 %fusion.20 = bf16[256,3,128]{0,2,1:T(8,128)(2,1)S(1)} fusion(bf16[8192,2,128]{0,2,1:T(8,128)(2,1)S(1)} %copy-done.7, f32[3,256,8192]{2,1,0:T(8,128)} %get-tuple-element.16, f32[3,256]{1,0:T(4,128)S(1)} %broadcast_maximum_fusion, pred[256,8192]{1,0:T(8,128)(4,1)S(1)} %fusion.11, f32[256,3]{0,1:T(4,128)S(1)} %bitcast.110), kind=kOutput, calls=%fused_computation.34 | convolution fusion | flops 1635975168 | bytes 29564928 | tf_op jit(solution)/shard_map/hqk,kd->hqd/dot_general | solution.py:60
  206.8 34.1 %all-gather.8.cloned.1.call-done = bf16[384,1536]{0,1:T(8,128)(2,1)} async-done(((bf16[384,48]{0,1:T(8,128)(2,1)}), bf16[384,1536]{0,1:T(8,128)(2,1)}) %all-gather.8.cloned.1.call-update) | async-done | bytes 1179664 | tf_op jit(solution)/shard_map/all_gather | solution.py:116
  240.9 1.9 convolution_convert_fusion
  242.8 1.2 copy.56
  244.0 0.1 copy.48
  244.1 0.1 eq.49
  244.3 0.1 eq.45
  244.4 9.0 %reduce-window.6 = s32[32,8,128]{2,1,0:T(8,128)S(1)} reduce-window(s32[32,8,128]{2,1,0:T(8,128)S(1)} %fusion.38, s32[]{:T(128)} %constant.26.clone.1), window={size=1x1x128 pad=0_0x0_0x127_0}, to_apply=%region_4.5 | reduce-window | flops 4161536 | bytes 262148 | tf_op jit(solution)/shard_map/reduce-window
  253.4 0.1 slice.65
  253.5 0.1 copy.50
  253.7 0.1 copy.51
  253.8 0.1 copy.47
  253.9 0.1 mul.183
  254.1 0.1 broadcast_add_fusion
  254.2 5.9 %reduce-scatter.7.cloned.1.call-done = bf16[384,256]{1,0:T(8,128)(2,1)} async-done(((bf16[1536,256]{1,0:T(8,128)(2,1)}), bf16[384,256]{1,0:T(8,128)(2,1)}) %reduce-scatter.7.cloned.1.call-update) | async-done | bytes 196624
  260.1 1.1 copy.57
  261.2 0.1 fusion.26
  261.4 6.0 %psum.7 = f32[256]{0:T(256)S(1)} all-reduce(f32[256]{0:T(256)S(1)} %fusion.26), channel_id=1, replica_groups=mesh['seq'=32,'mp'=4] {'mp'}, use_global_device_ids=true, to_apply=%region_8.9 | all-reduce | flops 256 | bytes 2048 | tf_op jit(solution)/shard_map/psum | solution.py:123
  267.4 0.1 fusion.27
  267.5 8.9 %all_gather.19 = bf16[256,1536]{1,0:T(8,128)(2,1)S(1)} all-gather(bf16[256,384]{1,0:T(8,128)(2,1)S(1)} %fusion.27), channel_id=1, replica_groups=mesh['seq'=32,'mp'=4] {'mp'}, dimensions={1}, use_global_device_ids=true | all-gather | bytes 983040 | tf_op jit(solution)/shard_map/all_gather | solution.py:134
  276.4 19.7 %scatter_custom_fusion = bf16[2048,1536]{1,0:T(8,128)(2,1)} fusion(s32[1024]{0:T(1024)S(1)} %bitcast.107, bf16[256,1536]{1,0:T(8,128)(2,1)S(1)} %all_gather.19, s32[1024]{0:T(1024)S(1)} %broadcast_clamp_fusion.1, bf16[]{:T(256)} %constant.75.clone.1), kind=kCustom, calls=%fused_computation.19 | custom fusion | bytes 6291458 | tf_op jit(solution)/shard_map/scatter | solution.py:138
  296.1 83.9 %all_to_all.15 = bf16[32,64,1536]{2,1,0:T(8,128)(2,1)S(1)} all-to-all(bf16[32,64,1536]{2,1,0:T(8,128)(2,1)} %bitcast.94), channel_id=1, replica_groups=mesh['seq'=32,'mp'=4] {'seq'}, dimensions={0} | all-to-all | bytes 12582912 | tf_op jit(solution)/shard_map/all_to_all | solution.py:140
  380.0 2.7 copy-done.1
  382.6 3.2 fusion.24
  385.8 12.3 %convert_bitcast_fusion = bf16[32,1,64,1536]{3,2,0,1:T(8,128)(2,1)} fusion(f32[32,64,192]{2,1,0:T(8,128)} %fusion.24, bf16[32,64,1536]{2,1,0:T(8,128)(2,1)} %copy-done.1, bf16[1,192,1536]{2,1,0:T(8,128)(2,1)S(1)} %copy-done, bf16[1,192,1536]{2,1,0:T(8,128)(2,1)S(1)} %copy-done.9), kind=kOutput, calls=%fused_computation.18 | convolution fusion | flops 2420244480 | bytes 15335424 | tf_op jit(solution)/shard_map/secf,efd->secd/dot_general | solution.py:153
  398.1 18.4 %copy.58 = bf16[32,1,64,1536]{2,0,1,3:T(8,128)(2,1)} copy(bf16[32,1,64,1536]{3,2,0,1:T(8,128)(2,1)} %convert_bitcast_fusion) | data formatting | bytes 12582912
  416.5 17.9 %reshape.403 = bf16[1536,2048]{1,0:T(8,128)(2,1)} reshape(bf16[1536,1,32,64]{3,2,1,0:T(8,128)(2,1)} %bitcast.92) | data formatting | bytes 12582912
  434.4 60.5 %reduce-scatter.9.cloned.1.call-done = bf16[384,2048]{1,0:T(8,128)(2,1)} async-done(((bf16[1536,2048]{1,0:T(8,128)(2,1)}), bf16[384,2048]{1,0:T(8,128)(2,1)}) %reduce-scatter.9.cloned.1.call-update) | async-done | bytes 1572880
  494.9 5.7 %reshape.404 = bf16[384,1,32,64]{3,2,1,0:T(8,128)(2,1)} reshape(bf16[384,2048]{1,0:T(8,128)(2,1)} %reduce-scatter.9.cloned.1.call-done) | data formatting | bytes 3145728
  500.6 5.5 copy.59
  506.1 9.4 %all-to-all-start.2 = ((bf16[32,64,384]{2,1,0:T(8,128)(2,1)}), bf16[32,64,384]{2,1,0:T(8,128)(2,1)S(1)}, u32[]{:S(2)}, u32[]{:S(2)}) async-start(bf16[32,64,384]{2,1,0:T(8,128)(2,1)} %bitcast.96), calls=%async_computation.2 | async-start | bytes 3145728 | tf_op jit(solution)/shard_map/all_to_all | solution.py:160
  515.5 0.1 copy.52
  515.7 23.2 %all-to-all-done.2 = bf16[32,64,384]{2,1,0:T(8,128)(2,1)S(1)} async-done(((bf16[32,64,384]{2,1,0:T(8,128)(2,1)}), bf16[32,64,384]{2,1,0:T(8,128)(2,1)S(1)}, u32[]{:S(2)}, u32[]{:S(2)}) %all-to-all-start.2) | async-done | bytes 1572896 | tf_op jit(solution)/shard_map/all_to_all | solution.py:160
  538.9 3.9 gather_fusion
  542.8 0.4 reshape.371
  543.2 1.0 multiply_reduce_fusion
  544.2 0.7 fusion.28
  (46 shorter events, 0.5 us)
Async XLA Ops:
  6.5 379.3 %copy-start = (bf16[1,192,1536]{2,1,0:T(8,128)(2,1)S(1)}, bf16[1,192,1536]{2,1,0:T(8,128)(2,1)}, u32[]{:S(2)}) copy-start(bf16[1,192,1536]{2,1,0:T(8,128)(2,1)} %param.19) | copy-start | bytes 1769476
  6.5 13.8 %copy-start.6 = (s32[3]{0:T(128)S(1)}, s32[3]{0:T(128)}, u32[]{:S(2)}) copy-start(s32[3]{0:T(128)} %param.14) | copy-start | bytes 40
  6.5 16.4 %copy-start.2 = (bf16[256,384]{1,0:T(8,128)(2,1)S(1)}, bf16[256,384]{1,0:T(8,128)(2,1)}, u32[]{:S(2)}) copy-start(bf16[256,384]{1,0:T(8,128)(2,1)} %param.10) | copy-start | bytes 589828
  6.5 83.6 %all-gather.4.cloned.1.call-start = ((), (), s32[]{:S(2)}) async-start(), calls=%async_computation.5 | async-start | bytes 1216512 | tf_op jit(solution)/shard_map/all_gather | solution.py:78
  9.4 34.4 %all-to-all-start = ((bf16[32,48,512]{2,1,0:T(8,128)(2,1)}), bf16[32,48,512]{2,1,0:T(8,128)(2,1)S(1)}, u32[]{:S(2)}, u32[]{:S(2)}) async-start(bf16[32,48,512]{2,1,0:T(8,128)(2,1)} %stack.4), calls=%async_computation | async-start | bytes 3145728 | tf_op jit(solution)/shard_map/all_to_all | solution.py:83
  20.3 149.9 %all-gather.6.cloned.1.call-start = ((), (), s32[]{:S(2)}) async-start(), calls=%async_computation.6 | async-start | bytes 4325376 | tf_op jit(solution)/shard_map/all_gather | solution.py:106
  45.7 195.1 %all-gather.8.cloned.1.call-start = ((), (), s32[]{:S(2)}) async-start(), calls=%async_computation.7 | async-start | bytes 1216512 | tf_op jit(solution)/shard_map/all_gather | solution.py:116
  46.5 213.6 %reduce-scatter.7.cloned.1.call-start = ((), (), s32[]{:S(2)}) async-start(), calls=%async_computation.8 | async-start | bytes 983040
  182.4 12.5 %copy-start.7 = (bf16[8192,2,128]{0,2,1:T(8,128)(2,1)S(1)}, bf16[8192,2,128]{0,2,1:T(8,128)(2,1)}, u32[]{:S(2)}) copy-start(bf16[8192,2,128]{0,2,1:T(8,128)(2,1)} %all-gather.6.cloned.1.call-done) | copy-start | bytes 12582916
  206.8 37.2 %copy-start.5 = (s32[256,4]{0,1:T(4,128)S(1)}, s32[256,4]{0,1:T(4,128)}, u32[]{:S(2)}) copy-start(s32[256,4]{0,1:T(4,128)} %param.15) | copy-start | bytes 12292
  206.8 54.4 %copy-start.3 = (bf16[256,384]{1,0:T(8,128)(2,1)S(1)}, bf16[256,384]{1,0:T(8,128)(2,1)}, u32[]{:S(2)}) copy-start(bf16[256,384]{1,0:T(8,128)(2,1)} %param.10) | copy-start | bytes 589828
  243.9 251.0 %reduce-scatter.9.cloned.1.call-start = ((), (), s32[]{:S(2)}) async-start(), calls=%async_computation.9 | async-start | bytes 7864320
  296.1 86.5 %copy-start.8 = (bf16[1,192,1536]{2,1,0:T(8,128)(2,1)S(1)}, bf16[1,192,1536]{2,1,0:T(8,128)(2,1)}, u32[]{:S(2)}) copy-start(bf16[1,192,1536]{2,1,0:T(8,128)(2,1)} %param.17) | copy-start | bytes 1769476
  380.0 2.7 copy-start.1
  382.6 3.2 copy-start.9
  500.6 14.9 %copy-start.4 = (f32[256,4]{0,1:T(4,128)S(1)}, f32[256,4]{0,1:T(4,128)}, u32[]{:S(2)}) copy-start(f32[256,4]{0,1:T(4,128)} %param.16) | copy-start | bytes 12292
  506.1 32.8 %all-to-all-start.2 = ((bf16[32,64,384]{2,1,0:T(8,128)(2,1)}), bf16[32,64,384]{2,1,0:T(8,128)(2,1)S(1)}, u32[]{:S(2)}, u32[]{:S(2)}) async-start(bf16[32,64,384]{2,1,0:T(8,128)(2,1)} %bitcast.96), calls=%async_computation.2 | async-start | bytes 3145728 | tf_op jit(solution)/shard_map/all_to_all | solution.py:160
Sparse Core Ops, SparseCore 0:
  10.3 79.8 all-gather.3
  92.9 77.2 all-gather.5
  173.2 67.6 all-gather.7
  244.1 16.0 reduce-scatter.6
  434.6 60.3 reduce-scatter.8
